TPU v7x, 512 devices: a whole 4x8x8 slice. The times are simulated.
512 devices in a mesh: ctx: 32 (over y, x), fsdp: 16 (over z, core).
Axes of the slice: x: 4, y: 8, z: 8, core: 2. Of those that a mesh axis runs over, the one named last changes fastest.
Arguments:
- tokens: bfloat16 [131072, 4096], P(('ctx', 'fsdp')), may hold values from -48 to 48
- query_weight: bfloat16 [4096, 512], P('fsdp'), may hold values from -0.09375 to 0.09375
- key_weight: bfloat16 [4096, 128], P('fsdp'), may hold values from -0.09375 to 0.09375
- value_weight: bfloat16 [4096, 128], P('fsdp'), may hold values from -0.09375 to 0.09375
- chosen: int32 [256, 2], replicated, may hold values from 0 to 253, as said below
Outputs:
- attended: bfloat16 [131072, 512], P(('ctx', 'fsdp'))
Inputs may be any that keep to these rules, and one draw needn't show every extreme that they name: `chosen`: for query block q >= 3 both entries are distinct and below q - 1; block 2 names block 0 twice; blocks 0 and 1 name 0 twice, which selects nothing. The last block always selects block 253.
All inputs are finite; a program needn't handle non-finite values.
Results may differ from a plain program's by a relative error of at most 0.0065.
The roundings to bfloat16 on the way count: a program that leaves them out, or rounds other values in their place, can miss the bound.
Values may be sent and summed in bfloat16 or wider, within the bound.
No kernel may reach another device: no remote copies, remote signals or barrier semaphores. Data moves between devices by JAX's collectives and lax.ppermute only.
A program may use at most 64 MiB of HBM per device.

v0:
```python
import jax
import jax.numpy as jnp
from jax import lax
from jax.sharding import Mesh, PartitionSpec as P

QH = 4


def from_behind(array, axis, by):
    peers = lax.axis_size(axis)
    pairs = [(i, i + by) for i in range(peers) if 0 <= i + by < peers]
    return lax.ppermute(array, axis, pairs)


def gather_rows(array, axis):
    peers = lax.axis_size(axis)
    spread = jnp.broadcast_to(array[None], (peers,) + array.shape)
    got = lax.all_to_all(spread, axis, split_axis=0, concat_axis=0, tiled=True)
    return got.reshape((peers * array.shape[0],) + array.shape[1:])


def ring_gather_rows(array, axis, early_steps, tied):
    peers = lax.axis_size(axis)
    chips = peers // 2
    shift_pairs = lambda by: [(i, (i + by) % peers) for i in range(peers)]
    ahead = array
    behind = array
    from_ahead = []
    from_behind_ = []
    for step in range(chips // 2):
        if step == early_steps:
            ahead, behind, tied = lax.optimization_barrier((ahead, behind, tied))
            from_ahead[-1] = ahead
            if from_behind_:
                from_behind_[-1] = behind
        ahead = lax.ppermute(ahead, axis, shift_pairs(2))
        from_ahead.append(ahead)
        if step < chips // 2 - 1:
            behind = lax.ppermute(behind, axis, shift_pairs(-2))
            from_behind_.append(behind)
    mine = jnp.stack(from_ahead[::-1] + [array] + from_behind_, axis=0)
    other = lax.ppermute(mine, axis, [(i, i ^ 1) for i in range(peers)])
    lane = lax.axis_index(axis)
    start = (lane // 2 - chips // 2) % chips

    def natural(stacked):
        doubled = jnp.concatenate([stacked, stacked], axis=0)
        return lax.dynamic_slice_in_dim(doubled, chips - start, chips, 0)

    mine, other = (natural(mine), natural(other))
    core = lane % 2
    first = jnp.where(core == 0, mine, other)
    second = jnp.where(core == 0, other, mine)
    full = jnp.stack([first, second], axis=1)
    return (full.reshape((peers * array.shape[0],) + array.shape[1:]), tied)


def swap_partner(array, axis):
    peers = lax.axis_size(axis)
    pairs = [(i, i ^ 1) for i in range(peers)]
    return lax.ppermute(array, axis, pairs)


def per_device(tokens, query_weight, key_weight, value_weight, chosen):
    token_rows = tokens.shape[0]
    head_width = key_weight.shape[1]
    lane_count = lax.axis_size("fsdp")
    lane_index = lax.axis_index("fsdp")
    group_index = lax.axis_index(("cy", "cx"))
    blocks_group = lane_count // 2
    my_block = group_index * blocks_group + lane_index // 2
    global_index = group_index * lane_count + lane_index
    kv_weight = lax.all_gather(
        jnp.concatenate([key_weight, value_weight], axis=1), "fsdp", axis=0, tiled=True
    )
    q_weight, kv_weight = ring_gather_rows(query_weight, "fsdp", 2, kv_weight)
    kv_f32 = jnp.dot(tokens, kv_weight, preferred_element_type=jnp.float32)
    key_value = kv_f32.astype(jnp.bfloat16)
    along_x = lax.all_gather(key_value[None], "cx", axis=0, tiled=True)
    candidates = lax.all_gather(along_x[None], "cy", axis=0, tiled=True).reshape(
        (-1,) + key_value.shape
    )
    before_pair = from_behind(key_value, ("cy", "cx", "fsdp"), 1)
    own_block = jnp.concatenate([before_pair, key_value], axis=0)
    queries = jnp.dot(tokens, q_weight, preferred_element_type=jnp.float32)
    queries = queries.astype(jnp.bfloat16).reshape(token_rows, QH, head_width)
    queries, chosen = lax.optimization_barrier((queries, chosen))
    dest_block = group_index * blocks_group + jnp.arange(lane_count, dtype=jnp.int32) // 2
    dest_pick = chosen[dest_block, jnp.arange(lane_count, dtype=jnp.int32) % 2]
    outgoing = jnp.take(candidates, dest_pick // blocks_group, axis=0, mode="clip")
    incoming = lax.all_to_all(outgoing, "fsdp", split_axis=0, concat_axis=0, tiled=True)
    mine = lax.dynamic_index_in_dim(chosen, my_block, 0, keepdims=False)
    my_choice = lane_index % 2
    my_pick = jnp.where(my_choice == 0, mine[0], mine[1])
    place = my_pick % blocks_group * 2
    block_mine = lax.dynamic_slice_in_dim(incoming, place, 2, 0).reshape(
        2 * token_rows, 2 * head_width
    )
    block_partner = swap_partner(block_mine, "fsdp")
    scale = head_width ** (-0.5)
    scores = (
        jnp.concatenate(
            [
                jnp.einsum(
                    "qhd,kd->hqk", queries, rows[:, :head_width], preferred_element_type=jnp.float32
                )
                for rows in (own_block, block_mine, block_partner)
            ],
            axis=2,
        )
        * scale
    )
    value_rows = jnp.concatenate(
        [own_block[:, head_width:], block_mine[:, head_width:], block_partner[:, head_width:]],
        axis=0,
    )
    window_rows = own_block.shape[0]
    pick_rows = block_mine.shape[0]
    row_index = jnp.arange(token_rows, dtype=jnp.int32)
    column = jnp.arange(window_rows, dtype=jnp.int32)
    causal = (column[None, :] <= row_index[:, None] + token_rows) & (
        (column[None, :] >= token_rows) | (global_index > 0)
    )
    first_ok = mine[0] < my_block - 1
    second_ok = (mine[1] < my_block - 1) & (mine[1] != mine[0])
    mine_ok = jnp.where(my_choice == 0, first_ok, second_ok)
    partner_ok = jnp.where(my_choice == 0, second_ok, first_ok)
    visible = jnp.concatenate(
        [
            causal,
            jnp.broadcast_to(mine_ok, (token_rows, pick_rows)),
            jnp.broadcast_to(partner_ok, (token_rows, pick_rows)),
        ],
        axis=1,
    )
    scores = jnp.where(visible[None], scores, -jnp.inf)
    highest = jnp.max(scores, axis=2, keepdims=True)
    probs = jnp.exp(scores - highest)
    denominator = jnp.sum(probs, axis=2, keepdims=True)
    mixed = (
        jnp.einsum(
            "hqk,kd->hqd",
            probs.astype(jnp.bfloat16),
            value_rows,
            preferred_element_type=jnp.float32,
        )
        / denominator
    )
    return jnp.transpose(mixed, (1, 0, 2)).reshape(token_rows, -1).astype(jnp.bfloat16)


def split_ctx(mesh):
    column = mesh.devices[:, 0]
    coords = [getattr(device, "coords", None) for device in column]
    if any((c is None for c in coords)):
        across = 1
    else:
        across = len({c[0] for c in coords})
    groups, lanes = mesh.devices.shape
    return Mesh(mesh.devices.reshape(groups // across, across, lanes), ("cy", "cx", "fsdp"))


def solution(mesh):
    split = split_ctx(mesh)
    rows = P(("cy", "cx", "fsdp"), None)
    return jax.shard_map(
        per_device,
        mesh=split,
        in_specs=(rows, P("fsdp", None), P("fsdp", None), P("fsdp", None), P()),
        out_specs=rows,
        check_vma=False,
    )
```

profile of v0, /device:TPU:7, one launch (start us, length us, event | category | flops | bytes accessed | tf_op | source)
XLA Modules:
  0.0 211.8 jit_solution(5109586770303646003)
XLA Ops:
  6.5 1.7 pad_maximum_fusion.2
  8.2 0.0 all-gather.5.cloned.1.call-update
  8.3 0.0 copy-start.3
  8.3 0.0 all-gather.7.cloned.1.call-start
  8.3 4.1 %collective-permute-start = (bf16[256,512]{1,0:T(8,128)(2,1)}, bf16[256,512]{1,0:T(8,128)(2,1)S(1)}, u32[]{:S(2)}, u32[]{:S(2)}) collective-permute-start(bf16[256,512]{1,0:T(8,128)(2,1)} %param.6), channel_id=1, source_target_pairs={{0,2},{1,3},{2,4},{3,5},{4,6},{5,7},{6,8},{7,9},{8,10},{9,11},{10,... | collective-permute-start | bytes 786440 | tf_op jit(solution)/shard_map/ppermute | solution.py:36
  12.5 8.6 %collective-permute-start.2 = (bf16[256,512]{1,0:T(8,128)(2,1)}, bf16[256,512]{1,0:T(8,128)(2,1)S(1)}, u32[]{:S(2)}, u32[]{:S(2)}) collective-permute-start(bf16[256,512]{1,0:T(8,128)(2,1)} %param.6), channel_id=1, source_target_pairs={{0,14},{1,15},{2,0},{3,1},{4,2},{5,3},{6,4},{7,5},{8,6},{9,7},{10,... | collective-permute-start | bytes 786440 | tf_op jit(solution)/shard_map/ppermute | solution.py:39
  21.1 4.3 %collective-permute-done = bf16[256,512]{1,0:T(8,128)(2,1)S(1)} collective-permute-done((bf16[256,512]{1,0:T(8,128)(2,1)}, bf16[256,512]{1,0:T(8,128)(2,1)S(1)}, u32[]{:S(2)}, u32[]{:S(2)}) %collective-permute-start) | collective-permute-done | bytes 262176 | tf_op jit(solution)/shard_map/ppermute | solution.py:36
  25.4 1.9 collective-permute-start.1
  27.3 4.6 %collective-permute-start.3 = (bf16[256,512]{1,0:T(8,128)(2,1)S(1)}, bf16[256,512]{1,0:T(8,128)(2,1)S(1)}, u32[]{:S(2)}, u32[]{:S(2)}) collective-permute-start(bf16[256,512]{1,0:T(8,128)(2,1)S(1)} %collective-permute-done.2), channel_id=1, source_target_pairs={{0,14},{1,15},{2,0},{3,1},{4,2},{5,3},{6,4},{7,5},{8,6},{9,7},{10,... | collective-permute-start | bytes 786440 | tf_op jit(solution)/shard_map/ppermute | solution.py:39
  31.9 5.2 %collective-permute-done.1 = bf16[256,512]{1,0:T(8,128)(2,1)S(1)} collective-permute-done((bf16[256,512]{1,0:T(8,128)(2,1)S(1)}, bf16[256,512]{1,0:T(8,128)(2,1)S(1)}, u32[]{:S(2)}, u32[]{:S(2)}) %collective-permute-start.1) | collective-permute-done | bytes 262176 | tf_op jit(solution)/shard_map/ppermute | solution.py:36
  37.0 0.2 collective-permute-done.3
  37.2 20.6 %all-gather.5.cloned.1.call-done = bf16[4096,256]{1,0:T(8,128)(2,1)} async-done(((bf16[256,256]{1,0:T(8,128)(2,1)}), bf16[4096,256]{1,0:T(8,128)(2,1)}) %all-gather.5.cloned.1.call-update) | async-done | bytes 2097168 | tf_op jit(solution)/shard_map/all_gather | solution.py:73
  57.8 2.3 %fusion.16 = bf16[256,256]{1,0:T(8,128)(2,1)S(1)} fusion(bf16[256,4096]{1,0:T(8,128)(2,1)S(1)} %copy-done, bf16[4096,256]{1,0:T(8,128)(2,1)} %all-gather.5.cloned.1.call-done), kind=kOutput, calls=%fused_computation.24 | convolution fusion | flops 536936448 | bytes 4325376 | tf_op jit(solution)/shard_map/dot_general | solution.py:77
  60.1 10.6 %all-gather = bf16[1024,256]{1,0:T(8,128)(2,1)} all-gather(bf16[256,256]{1,0:T(8,128)(2,1)S(1)} %fusion.16), channel_id=2, replica_groups=mesh['cy'=8,'cx'=4,'fsdp'=16] {'cx'}, dimensions={0}, use_global_device_ids=true | all-gather | bytes 655360 | tf_op jit(solution)/shard_map/all_gather | solution.py:79
  70.8 0.0 all-gather.7.cloned.1.call-update
  70.8 3.0 %collective-permute-start.4 = (bf16[256,512]{1,0:T(8,128)(2,1)S(1)}, bf16[256,512]{1,0:T(8,128)(2,1)S(1)}, u32[]{:S(2)}, u32[]{:S(2)}) collective-permute-start(bf16[256,512]{1,0:T(8,128)(2,1)S(1)} %collective-permute-done.1), channel_id=1, source_target_pairs={{0,2},{1,3},{2,4},{3,5},{4,6},{5,7},{6,8},{7,9},{8,10},{9,11},{10,... | collective-permute-start | bytes 786440 | tf_op jit(solution)/shard_map/ppermute | solution.py:36
  73.8 5.3 %collective-permute-done.4 = bf16[256,512]{1,0:T(8,128)(2,1)S(1)} collective-permute-done((bf16[256,512]{1,0:T(8,128)(2,1)S(1)}, bf16[256,512]{1,0:T(8,128)(2,1)S(1)}, u32[]{:S(2)}, u32[]{:S(2)}) %collective-permute-start.4) | collective-permute-done | bytes 262176 | tf_op jit(solution)/shard_map/ppermute | solution.py:36
  79.1 1.9 collective-permute-start.5
  81.0 4.6 %collective-permute-start.6 = (bf16[256,512]{1,0:T(8,128)(2,1)S(1)}, bf16[256,512]{1,0:T(8,128)(2,1)S(1)}, u32[]{:S(2)}, u32[]{:S(2)}) collective-permute-start(bf16[256,512]{1,0:T(8,128)(2,1)S(1)} %collective-permute-done.3), channel_id=1, source_target_pairs={{0,14},{1,15},{2,0},{3,1},{4,2},{5,3},{6,4},{7,5},{8,6},{9,7},{10,... | collective-permute-start | bytes 786440 | tf_op jit(solution)/shard_map/ppermute | solution.py:39
  85.6 1.8 collective-permute-done.5
  87.4 0.9 bitcast_dynamic-update-slice_fusion.22
  88.3 0.8 bitcast_dynamic-update-slice_fusion.19
  89.1 0.8 bitcast_dynamic-update-slice_fusion.16
  90.0 0.8 bitcast_dynamic-update-slice_fusion.13
  90.8 0.8 bitcast_dynamic-update-slice_fusion.10
  91.6 0.8 bitcast_dynamic-update-slice_fusion.7
  92.5 0.8 bitcast_dynamic-update-slice_fusion.4
  93.3 0.0 collective-permute-done.6
  93.3 0.7 copy-done.4
  94.0 0.8 bitcast_dynamic-update-slice_fusion.1
  94.9 7.6 %collective-permute-start.7 = (bf16[8,256,512]{2,1,0:T(8,128)(2,1)}, bf16[8,256,512]{2,1,0:T(8,128)(2,1)}, u32[]{:S(2)}, u32[]{:S(2)}) collective-permute-start(bf16[8,256,512]{2,1,0:T(8,128)(2,1)} %get-tuple-element.17), channel_id=1, source_target_pairs={{0,1},{1,0},{2,3},{3,2},{4,5},{5,4},{6,7},{7,6},{8,9},{9,8},{10,11... | collective-permute-start | bytes 6291464 | tf_op jit(solution)/shard_map/ppermute | solution.py:42
  102.5 1.7 bitcast_dynamic-update-slice_fusion.23
  104.2 1.7 bitcast_dynamic-update-slice_fusion.20
  105.9 0.7 bitcast_dynamic-update-slice_fusion.17
  106.6 0.7 bitcast_dynamic-update-slice_fusion.14
  107.3 0.7 bitcast_dynamic-update-slice_fusion.11
  108.0 0.7 bitcast_dynamic-update-slice_fusion.8
  108.7 0.7 bitcast_dynamic-update-slice_fusion.5
  109.5 1.7 bitcast_dynamic-update-slice_fusion.2
  111.2 0.0 collective-permute-done.7
  111.2 4.5 %select_bitcast_fusion.1 = (bf16[8,1,256,512]{3,2,1,0:T(8,128)(2,1)S(1)}, bf16[8,1,256,512]{3,2,1,0:T(8,128)(2,1)S(1)}) fusion(pred[]{:T(512)S(6)} %eq.14, bf16[16,256,512]{2,1,0:T(8,128)(2,1)} %bitcast_dynamic-update-slice_fusion.2, s32[]{:T(128)S(6)} %select_n.118, bf16[8,256,512]{2,1,0:T(8,128)(2,1)} %collective-permute-done.7), kind=kLoop, calls=%fused_computation.14 | loop fusion | flops 4194304 | bytes 8388613 | tf_op jit(solution)/shard_map/stack | solution.py:54
  115.7 0.4 pad_maximum_fusion
  116.1 0.0 copy-start.1
  116.1 1.3 convolution_convert_fusion
  117.4 0.7 gather_fusion
  118.2 11.0 %all-gather.7.cloned.1.call-done = bf16[32,256,256]{2,1,0:T(8,128)(2,1)} async-done(((bf16[4,256,256]{2,1,0:T(8,128)(2,1)}), bf16[32,256,256]{2,1,0:T(8,128)(2,1)}) %all-gather.7.cloned.1.call-update) | async-done | bytes 4194320 | tf_op jit(solution)/shard_map/all_gather | solution.py:80
  129.2 4.2 %gather_fusion.1 = bf16[16,256,256]{2,1,0:T(8,128)(2,1)} fusion(bf16[32,256,256]{2,1,0:T(8,128)(2,1)} %all-gather.7.cloned.1.call-done, s32[1024]{0:T(1024)S(1)} %pad_clamp_fusion), kind=kCustom, calls=%fused_computation.1 | custom fusion | bytes 4194368 | tf_op jit(solution)/shard_map/jit(_take)/gather | solution.py:90
  133.4 8.1 %all-to-all-start = ((bf16[16,256,256]{2,1,0:T(8,128)(2,1)}), bf16[16,256,256]{2,1,0:T(8,128)(2,1)}, u32[]{:S(2)}, u32[]{:S(2)}) async-start(bf16[16,256,256]{2,1,0:T(8,128)(2,1)} %gather_fusion.1), calls=%async_computation | async-start | bytes 4194304 | tf_op jit(solution)/shard_map/all_to_all | solution.py:91
  141.5 0.1 fusion.19
  141.6 3.5 %collective-permute-start.8 = (bf16[256,256]{1,0:T(8,128)(2,1)S(1)}, bf16[256,256]{1,0:T(8,128)(2,1)S(1)}, u32[]{:S(2)}, u32[]{:S(2)}) collective-permute-start(bf16[256,256]{1,0:T(8,128)(2,1)S(1)} %fusion.16), channel_id=1, source_target_pairs={{0,1},{1,2},{2,3},{3,4},{4,5},{5,6},{6,7},{7,8},{8,9},{9,10},{10,1... | collective-permute-start | bytes 393224 | tf_op jit(solution)/shard_map/ppermute | solution.py:12
  145.2 0.1 constant_dynamic-slice_fusion.1
  145.3 0.5 fusion.43
  149.5 39.2 %collective-permute-done.8 = bf16[256,256]{1,0:T(8,128)(2,1)S(1)} collective-permute-done((bf16[256,256]{1,0:T(8,128)(2,1)S(1)}, bf16[256,256]{1,0:T(8,128)(2,1)S(1)}, u32[]{:S(2)}, u32[]{:S(2)}) %collective-permute-start.8) | collective-permute-done | bytes 131104 | tf_op jit(solution)/shard_map/ppermute | solution.py:12
  188.7 1.7 convolution_bitcast_fusion.2
  190.4 1.4 add_add_fusion
  191.8 1.1 constant_dynamic-slice_fusion
  193.0 5.8 %collective-permute-start.9 = (bf16[512,256]{1,0:T(8,128)(2,1)S(1)}, bf16[512,256]{1,0:T(8,128)(2,1)S(1)}, u32[]{:S(2)}, u32[]{:S(2)}) collective-permute-start(bf16[512,256]{1,0:T(8,128)(2,1)S(1)} %bitcast.100), channel_id=1, source_target_pairs={{0,1},{1,0},{2,3},{3,2},{4,5},{5,4},{6,7},{7,6},{8,9},{9,8},{10,11... | collective-permute-start | bytes 786440 | tf_op jit(solution)/shard_map/ppermute | solution.py:61
  198.8 0.4 convolution_bitcast_fusion.1
  199.2 0.7 collective-permute-done.9
  199.9 0.4 convolution_bitcast_fusion
  200.3 0.8 fusion.18
  201.1 1.4 fusion.1
  202.5 1.6 fusion.13
  204.1 0.8 copy.25
  (25 shorter events, 0.1 us)
Async XLA Ops:
  6.5 51.3 %copy-start = (bf16[256,4096]{1,0:T(8,128)(2,1)S(1)}, bf16[256,4096]{1,0:T(8,128)(2,1)}, u32[]{:S(2)}) copy-start(bf16[256,4096]{1,0:T(8,128)(2,1)} %param.5) | copy-start | bytes 6291460
  6.5 51.3 %all-gather.5.cloned.1.call-start = ((), (), s32[]{:S(2)}) async-start(), calls=%async_computation.1 | async-start | bytes 2228224 | tf_op jit(solution)/shard_map/all_gather | solution.py:73
  8.3 82.6 %copy-start.3 = (bf16[256,512]{1,0:T(8,128)(2,1)S(1)}, bf16[256,512]{1,0:T(8,128)(2,1)}, u32[]{:S(2)}) copy-start(bf16[256,512]{1,0:T(8,128)(2,1)} %param.6) | copy-start | bytes 786436
  8.3 120.9 %all-gather.7.cloned.1.call-start = ((), (), s32[]{:S(2)}) async-start(), calls=%async_computation.2 | async-start | bytes 4718592 | tf_op jit(solution)/shard_map/all_gather | solution.py:80
  8.3 17.0 %collective-permute-start = (bf16[256,512]{1,0:T(8,128)(2,1)}, bf16[256,512]{1,0:T(8,128)(2,1)S(1)}, u32[]{:S(2)}, u32[]{:S(2)}) collective-permute-start(bf16[256,512]{1,0:T(8,128)(2,1)} %param.6), channel_id=1, source_target_pairs={{0,2},{1,3},{2,4},{3,5},{4,6},{5,7},{6,8},{7,9},{8,10},{9,11},{10,... | collective-permute-start | bytes 786440 | tf_op jit(solution)/shard_map/ppermute | solution.py:36
  12.5 14.8 %collective-permute-start.2 = (bf16[256,512]{1,0:T(8,128)(2,1)}, bf16[256,512]{1,0:T(8,128)(2,1)S(1)}, u32[]{:S(2)}, u32[]{:S(2)}) collective-permute-start(bf16[256,512]{1,0:T(8,128)(2,1)} %param.6), channel_id=1, source_target_pairs={{0,14},{1,15},{2,0},{3,1},{4,2},{5,3},{6,4},{7,5},{8,6},{9,7},{10,... | collective-permute-start | bytes 786440 | tf_op jit(solution)/shard_map/ppermute | solution.py:39
  25.4 11.7 %collective-permute-start.1 = (bf16[256,512]{1,0:T(8,128)(2,1)S(1)}, bf16[256,512]{1,0:T(8,128)(2,1)S(1)}, u32[]{:S(2)}, u32[]{:S(2)}) collective-permute-start(bf16[256,512]{1,0:T(8,128)(2,1)S(1)} %collective-permute-done), channel_id=1, source_target_pairs={{0,2},{1,3},{2,4},{3,5},{4,6},{5,7},{6,8},{7,9},{8,10},{9,11},{10,... | collective-permute-start | bytes 786440 | tf_op jit(solution)/shard_map/ppermute | solution.py:36
  27.3 9.9 %collective-permute-start.3 = (bf16[256,512]{1,0:T(8,128)(2,1)S(1)}, bf16[256,512]{1,0:T(8,128)(2,1)S(1)}, u32[]{:S(2)}, u32[]{:S(2)}) collective-permute-start(bf16[256,512]{1,0:T(8,128)(2,1)S(1)} %collective-permute-done.2), channel_id=1, source_target_pairs={{0,14},{1,15},{2,0},{3,1},{4,2},{5,3},{6,4},{7,5},{8,6},{9,7},{10,... | collective-permute-start | bytes 786440 | tf_op jit(solution)/shard_map/ppermute | solution.py:39
  70.8 8.3 %collective-permute-start.4 = (bf16[256,512]{1,0:T(8,128)(2,1)S(1)}, bf16[256,512]{1,0:T(8,128)(2,1)S(1)}, u32[]{:S(2)}, u32[]{:S(2)}) collective-permute-start(bf16[256,512]{1,0:T(8,128)(2,1)S(1)} %collective-permute-done.1), channel_id=1, source_target_pairs={{0,2},{1,3},{2,4},{3,5},{4,6},{5,7},{6,8},{7,9},{8,10},{9,11},{10,... | collective-permute-start | bytes 786440 | tf_op jit(solution)/shard_map/ppermute | solution.py:36
  79.1 15.8 %copy-start.5 = (bf16[256,512]{1,0:T(8,128)(2,1)}, bf16[256,512]{1,0:T(8,128)(2,1)S(1)}, u32[]{:S(2)}) copy-start(bf16[256,512]{1,0:T(8,128)(2,1)S(1)} %collective-permute-done.4) | copy-start | bytes 786436
  79.1 8.3 %collective-permute-start.5 = (bf16[256,512]{1,0:T(8,128)(2,1)S(1)}, bf16[256,512]{1,0:T(8,128)(2,1)S(1)}, u32[]{:S(2)}, u32[]{:S(2)}) collective-permute-start(bf16[256,512]{1,0:T(8,128)(2,1)S(1)} %collective-permute-done.4), channel_id=1, source_target_pairs={{0,2},{1,3},{2,4},{3,5},{4,6},{5,7},{6,8},{7,9},{8,10},{9,11},{10,... | collective-permute-start | bytes 786440 | tf_op jit(solution)/shard_map/ppermute | solution.py:36
  81.0 12.3 %collective-permute-start.6 = (bf16[256,512]{1,0:T(8,128)(2,1)S(1)}, bf16[256,512]{1,0:T(8,128)(2,1)S(1)}, u32[]{:S(2)}, u32[]{:S(2)}) collective-permute-start(bf16[256,512]{1,0:T(8,128)(2,1)S(1)} %collective-permute-done.3), channel_id=1, source_target_pairs={{0,14},{1,15},{2,0},{3,1},{4,2},{5,3},{6,4},{7,5},{8,6},{9,7},{10,... | collective-permute-start | bytes 786440 | tf_op jit(solution)/shard_map/ppermute | solution.py:39
  87.4 7.4 %copy-start.6 = (bf16[256,512]{1,0:T(8,128)(2,1)}, bf16[256,512]{1,0:T(8,128)(2,1)S(1)}, u32[]{:S(2)}) copy-start(bf16[256,512]{1,0:T(8,128)(2,1)S(1)} %collective-permute-done.5) | copy-start | bytes 786436
  93.3 0.7 copy-start.4
  94.9 16.3 %collective-permute-start.7 = (bf16[8,256,512]{2,1,0:T(8,128)(2,1)}, bf16[8,256,512]{2,1,0:T(8,128)(2,1)}, u32[]{:S(2)}, u32[]{:S(2)}) collective-permute-start(bf16[8,256,512]{2,1,0:T(8,128)(2,1)} %get-tuple-element.17), channel_id=1, source_target_pairs={{0,1},{1,0},{2,3},{3,2},{4,5},{5,4},{6,7},{7,6},{8,9},{9,8},{10,11... | collective-permute-start | bytes 6291464 | tf_op jit(solution)/shard_map/ppermute | solution.py:42
  116.1 1.3 copy-start.1
  133.4 58.4 %all-to-all-start = ((bf16[16,256,256]{2,1,0:T(8,128)(2,1)}), bf16[16,256,256]{2,1,0:T(8,128)(2,1)}, u32[]{:S(2)}, u32[]{:S(2)}) async-start(bf16[16,256,256]{2,1,0:T(8,128)(2,1)} %gather_fusion.1), calls=%async_computation | async-start | bytes 4194304 | tf_op jit(solution)/shard_map/all_to_all | solution.py:91
  141.6 47.0 %collective-permute-start.8 = (bf16[256,256]{1,0:T(8,128)(2,1)S(1)}, bf16[256,256]{1,0:T(8,128)(2,1)S(1)}, u32[]{:S(2)}, u32[]{:S(2)}) collective-permute-start(bf16[256,256]{1,0:T(8,128)(2,1)S(1)} %fusion.16), channel_id=1, source_target_pairs={{0,1},{1,2},{2,3},{3,4},{4,5},{5,6},{6,7},{7,8},{8,9},{9,10},{10,1... | collective-permute-start | bytes 393224 | tf_op jit(solution)/shard_map/ppermute | solution.py:12
  191.8 8.5 %copy-start.2 = (f32[4,256,512]{1,2,0:T(8,128)S(1)}, f32[4,256,512]{1,2,0:T(8,128)}, u32[]{:S(2)}) copy-start(f32[4,256,512]{1,2,0:T(8,128)} %convolution_bitcast_fusion.2) | copy-start | bytes 6291460
  193.0 6.9 %collective-permute-start.9 = (bf16[512,256]{1,0:T(8,128)(2,1)S(1)}, bf16[512,256]{1,0:T(8,128)(2,1)S(1)}, u32[]{:S(2)}, u32[]{:S(2)}) collective-permute-start(bf16[512,256]{1,0:T(8,128)(2,1)S(1)} %bitcast.100), channel_id=1, source_target_pairs={{0,1},{1,0},{2,3},{3,2},{4,5},{5,4},{6,7},{7,6},{8,9},{9,8},{10,11... | collective-permute-start | bytes 786440 | tf_op jit(solution)/shard_map/ppermute | solution.py:61
Sparse Core Ops, SparseCore 0:
  9.5 48.2 all-gather.4
  70.9 58.2 all-gather.6
where the time goes:
time: 212 us
  waiting for transfers between devices  88.3 us (42%)
  starting transfers between devices  53.7 us (25%)
  local copies, waits for them, and re-layouts  23.6 us (11%)
  between operations  17.4 us (8%)
  blocking collectives  10.6 us (5%)
  other arithmetic  10.4 us (5%)
  matrix products  7.73 us (4%)
    ppermute x1, waiting for transfers between devices, from_behind(): return lax.ppermute(array, axis, pairs)  39.2 us
    all_gather x1, waiting for transfers between devices, per_device(): lax.all_gather(jnp.concatenate([key_weight, value_weight], axis=1), 'fsdp...  20.6 us
    ppermute x3, starting transfers between devices, ring_gather_rows(): behind = lax.ppermute(behind, axis, shift_pairs(-2))  17.7 us
    ppermute x4, waiting for transfers between devices, ring_gather_rows(): ahead = lax.ppermute(ahead, axis, shift_pairs(2))  16.6 us
    unnamed x28, local copies, waits for them, and re-layouts  13.6 us
    all_gather x1, waiting for transfers between devices, per_device(): lax.all_gather(along_x[None], 'cy', axis=0, tiled=True)  11 us
    ppermute x4, starting transfers between devices, ring_gather_rows(): ahead = lax.ppermute(ahead, axis, shift_pairs(2))  11 us
    all_gather x1, blocking collectives, per_device(): along_x = lax.all_gather(key_value[None], 'cx', axis=0, tiled=True)  10.6 us
  transfers between devices with their start and end apart: 13, of which 9 were waited for; matrix products, arithmetic and copies ran while one was open for 13% of the time, Pallas kernels for 0%

commit v1 on v0

--- a/solution.py
+++ b/solution.py
@@ -4,6 +4,17 @@
 from jax.sharding import Mesh, PartitionSpec as P
 
 QH = 4
+
+
+def press_waves(vals):
+    n_all = jax.lax.axis_size("fsdp")
+    return jax.lax.all_to_all(
+        jnp.tile(vals, [n_all if nth == 0 else 1 for nth in range(vals.ndim)]),
+        "fsdp",
+        split_axis=0,
+        concat_axis=0,
+        tiled=True,
+    )
 
 
 def from_behind(array, axis, by):
@@ -70,9 +81,7 @@
     blocks_group = lane_count // 2
     my_block = group_index * blocks_group + lane_index // 2
     global_index = group_index * lane_count + lane_index
-    kv_weight = lax.all_gather(
-        jnp.concatenate([key_weight, value_weight], axis=1), "fsdp", axis=0, tiled=True
-    )
+    kv_weight = press_waves(jnp.concatenate([key_weight, value_weight], axis=1))
     q_weight, kv_weight = ring_gather_rows(query_weight, "fsdp", 2, kv_weight)
     kv_f32 = jnp.dot(tokens, kv_weight, preferred_element_type=jnp.float32)
     key_value = kv_f32.astype(jnp.bfloat16)

time: 212 us -> 244 us (1.15)
  waiting for transfers between devices: 88.3 us -> 113 us
  starting transfers between devices: 53.7 us -> 58.2 us
    ppermute x4, waiting for transfers between devices: 16.6 us -> 60.1 us  [ring_gather_rows(): ahead = lax.ppermute(ahead, axis, shift_pairs(2))]
    all_gather x1 -> x0, waiting for transfers between devices: 20.6 us -> none  [per_device(): lax.all_gather(jnp.concatenate([key_weight, value_weight], axis=1), 'fsdp...]
    all_to_all x0 -> x1, starting transfers between devices: none -> 11 us  [press_waves(): jax.lax.all_to_all(jnp.tile(vals, [n_all if nth == 0 else 1 for nth in ra...]
    ppermute x3, starting transfers between devices: 17.7 us -> 12.3 us  [ring_gather_rows(): behind = lax.ppermute(behind, axis, shift_pairs(-2))]
  transfers between devices with their start and end apart: 13 -> 13, of which waited for: 9 -> 8; matrix products, arithmetic and copies ran while one was open for 13% -> 11% of each run, Pallas kernels for 0% -> 0%
where the time goes in v1:
time: 244 us; the launch traced here: 243 us
  waiting for transfers between devices  113 us (46%)
  starting transfers between devices  58.2 us (24%)
  local copies, waits for them, and re-layouts  25.2 us (10%)
  between operations  17.6 us (7%)
  blocking collectives  11.3 us (5%)
  other arithmetic  9.71 us (4%)
  matrix products  7.73 us (3%)
    ppermute x4, waiting for transfers between devices, ring_gather_rows(): ahead = lax.ppermute(ahead, axis, shift_pairs(2))  60.1 us
    ppermute x1, waiting for transfers between devices, from_behind(): return lax.ppermute(array, axis, pairs)  39 us
    unnamed x28, local copies, waits for them, and re-layouts  13.6 us
    all_gather x1, waiting for transfers between devices, per_device(): lax.all_gather(along_x[None], 'cy', axis=0, tiled=True)  12.5 us
    ppermute x3, starting transfers between devices, ring_gather_rows(): behind = lax.ppermute(behind, axis, shift_pairs(-2))  12.3 us
    all_gather x1, blocking collectives, per_device(): along_x = lax.all_gather(key_value[None], 'cx', axis=0, tiled=True)  11.3 us
    all_to_all x1, starting transfers between devices, press_waves(): jax.lax.all_to_all(jnp.tile(vals, [n_all if nth == 0 else 1 for nth in ra...  11 us
    ppermute x4, starting transfers between devices, ring_gather_rows(): ahead = lax.ppermute(ahead, axis, shift_pairs(2))  9.03 us
  transfers between devices with their start and end apart: 13, of which 8 were waited for; matrix products, arithmetic and copies ran while one was open for 11% of the time, Pallas kernels for 0%

profile of v1, /device:TPU:7, one launch (start us, length us, event | category | flops | bytes accessed | tf_op | source)
XLA Modules:
  0.0 242.9 jit_solution(7440796818933710011)
XLA Ops:
  6.5 1.0 pad_maximum_fusion.2
  7.6 1.5 tile.2
  9.1 11.0 %all-to-all-start = ((bf16[16,256,256]{2,1,0:T(8,128)(2,1)}), bf16[16,256,256]{2,1,0:T(8,128)(2,1)}, u32[]{:S(2)}, u32[]{:S(2)}) async-start(bf16[16,256,256]{2,1,0:T(8,128)(2,1)} %tile.2), calls=%async_computation | async-start | bytes 4194304 | tf_op jit(solution)/shard_map/all_to_all | solution.py:11
  20.1 0.0 all-gather.4.cloned.1.call-start
  20.2 3.3 %collective-permute-start = (bf16[256,512]{1,0:T(8,128)(2,1)S(1)}, bf16[256,512]{1,0:T(8,128)(2,1)S(1)}, u32[]{:S(2)}, u32[]{:S(2)}) collective-permute-start(bf16[256,512]{1,0:T(8,128)(2,1)S(1)} %copy-done.3), channel_id=1, source_target_pairs={{0,2},{1,3},{2,4},{3,5},{4,6},{5,7},{6,8},{7,9},{8,10},{9,11},{10,... | collective-permute-start | bytes 786440 | tf_op jit(solution)/shard_map/ppermute | solution.py:47
  23.5 3.2 %collective-permute-start.2 = (bf16[256,512]{1,0:T(8,128)(2,1)S(1)}, bf16[256,512]{1,0:T(8,128)(2,1)S(1)}, u32[]{:S(2)}, u32[]{:S(2)}) collective-permute-start(bf16[256,512]{1,0:T(8,128)(2,1)S(1)} %copy-done.3), channel_id=1, source_target_pairs={{0,14},{1,15},{2,0},{3,1},{4,2},{5,3},{6,4},{7,5},{8,6},{9,7},{10,... | collective-permute-start | bytes 786440 | tf_op jit(solution)/shard_map/ppermute | solution.py:50
  26.7 47.6 %collective-permute-done = bf16[256,512]{1,0:T(8,128)(2,1)S(1)} collective-permute-done((bf16[256,512]{1,0:T(8,128)(2,1)S(1)}, bf16[256,512]{1,0:T(8,128)(2,1)S(1)}, u32[]{:S(2)}, u32[]{:S(2)}) %collective-permute-start) | collective-permute-done | bytes 262176 | tf_op jit(solution)/shard_map/ppermute | solution.py:47
  74.2 1.9 collective-permute-start.1
  76.1 0.0 collective-permute-done.2
  76.2 4.6 %collective-permute-start.3 = (bf16[256,512]{1,0:T(8,128)(2,1)S(1)}, bf16[256,512]{1,0:T(8,128)(2,1)S(1)}, u32[]{:S(2)}, u32[]{:S(2)}) collective-permute-start(bf16[256,512]{1,0:T(8,128)(2,1)S(1)} %collective-permute-done.2), channel_id=1, source_target_pairs={{0,14},{1,15},{2,0},{3,1},{4,2},{5,3},{6,4},{7,5},{8,6},{9,7},{10,... | collective-permute-start | bytes 786440 | tf_op jit(solution)/shard_map/ppermute | solution.py:50
  80.7 3.5 %collective-permute-done.1 = bf16[256,512]{1,0:T(8,128)(2,1)S(1)} collective-permute-done((bf16[256,512]{1,0:T(8,128)(2,1)S(1)}, bf16[256,512]{1,0:T(8,128)(2,1)S(1)}, u32[]{:S(2)}, u32[]{:S(2)}) %collective-permute-start.1) | collective-permute-done | bytes 262176 | tf_op jit(solution)/shard_map/ppermute | solution.py:47
  84.3 0.9 collective-permute-done.3
  85.2 0.0 all-to-all-done
  85.2 2.3 fusion.16
  87.5 11.3 %all-gather = bf16[1024,256]{1,0:T(8,128)(2,1)} all-gather(bf16[256,256]{1,0:T(8,128)(2,1)S(1)} %fusion.16), channel_id=2, replica_groups=mesh['cy'=8,'cx'=4,'fsdp'=16] {'cx'}, dimensions={0}, use_global_device_ids=true | all-gather | bytes 655360 | tf_op jit(solution)/shard_map/all_gather | solution.py:88
  98.8 0.0 all-gather.4.cloned.1.call-update
  98.8 1.9 collective-permute-start.4
  100.7 7.1 %collective-permute-done.4 = bf16[256,512]{1,0:T(8,128)(2,1)S(1)} collective-permute-done((bf16[256,512]{1,0:T(8,128)(2,1)S(1)}, bf16[256,512]{1,0:T(8,128)(2,1)S(1)}, u32[]{:S(2)}, u32[]{:S(2)}) %collective-permute-start.4) | collective-permute-done | bytes 262176 | tf_op jit(solution)/shard_map/ppermute | solution.py:47
  107.9 1.9 collective-permute-start.5
  109.8 4.6 %collective-permute-start.6 = (bf16[256,512]{1,0:T(8,128)(2,1)S(1)}, bf16[256,512]{1,0:T(8,128)(2,1)S(1)}, u32[]{:S(2)}, u32[]{:S(2)}) collective-permute-start(bf16[256,512]{1,0:T(8,128)(2,1)S(1)} %collective-permute-done.3), channel_id=1, source_target_pairs={{0,14},{1,15},{2,0},{3,1},{4,2},{5,3},{6,4},{7,5},{8,6},{9,7},{10,... | collective-permute-start | bytes 786440 | tf_op jit(solution)/shard_map/ppermute | solution.py:50
  114.4 1.8 collective-permute-done.5
  116.2 0.9 bitcast_dynamic-update-slice_fusion.22
  117.1 0.8 bitcast_dynamic-update-slice_fusion.19
  117.9 0.8 bitcast_dynamic-update-slice_fusion.16
  118.7 0.8 bitcast_dynamic-update-slice_fusion.13
  119.6 0.9 bitcast_dynamic-update-slice_fusion.10
  120.4 0.8 bitcast_dynamic-update-slice_fusion.7
  121.3 0.8 bitcast_dynamic-update-slice_fusion.4
  122.1 0.7 copy-done.4
  122.8 0.9 bitcast_dynamic-update-slice_fusion.1
  123.7 8.4 %collective-permute-start.7 = (bf16[8,256,512]{2,1,0:T(8,128)(2,1)}, bf16[8,256,512]{2,1,0:T(8,128)(2,1)}, u32[]{:S(2)}, u32[]{:S(2)}) collective-permute-start(bf16[8,256,512]{2,1,0:T(8,128)(2,1)} %get-tuple-element.17), channel_id=1, source_target_pairs={{0,1},{1,0},{2,3},{3,2},{4,5},{5,4},{6,7},{7,6},{8,9},{9,8},{10,11... | collective-permute-start | bytes 6291464 | tf_op jit(solution)/shard_map/ppermute | solution.py:53
  132.1 1.7 bitcast_dynamic-update-slice_fusion.23
  133.8 1.7 bitcast_dynamic-update-slice_fusion.20
  135.5 0.7 bitcast_dynamic-update-slice_fusion.17
  136.2 0.7 bitcast_dynamic-update-slice_fusion.14
  136.9 0.7 bitcast_dynamic-update-slice_fusion.11
  137.6 0.7 bitcast_dynamic-update-slice_fusion.8
  138.4 0.7 bitcast_dynamic-update-slice_fusion.5
  139.1 1.7 bitcast_dynamic-update-slice_fusion.2
  140.8 0.0 collective-permute-done.7
  140.8 4.5 %select_bitcast_fusion.1 = (bf16[8,1,256,512]{3,2,1,0:T(8,128)(2,1)S(1)}, bf16[8,1,256,512]{3,2,1,0:T(8,128)(2,1)S(1)}) fusion(pred[]{:T(512)S(6)} %eq.14, bf16[16,256,512]{2,1,0:T(8,128)(2,1)} %bitcast_dynamic-update-slice_fusion.2, s32[]{:T(128)S(6)} %select_n.118, bf16[8,256,512]{2,1,0:T(8,128)(2,1)} %collective-permute-done.7), kind=kLoop, calls=%fused_computation.14 | loop fusion | flops 4194304 | bytes 8388613 | tf_op jit(solution)/shard_map/stack | solution.py:65
  145.4 0.4 pad_maximum_fusion
  145.8 0.0 copy-start.1
  145.8 1.3 convolution_convert_fusion
  147.1 0.7 gather_fusion
  147.8 12.5 %all-gather.4.cloned.1.call-done = bf16[32,256,256]{2,1,0:T(8,128)(2,1)} async-done(((bf16[4,256,256]{2,1,0:T(8,128)(2,1)}), bf16[32,256,256]{2,1,0:T(8,128)(2,1)}) %all-gather.4.cloned.1.call-update) | async-done | bytes 4194320 | tf_op jit(solution)/shard_map/all_gather | solution.py:89
  160.3 4.2 %gather_fusion.1 = bf16[16,256,256]{2,1,0:T(8,128)(2,1)} fusion(bf16[32,256,256]{2,1,0:T(8,128)(2,1)} %all-gather.4.cloned.1.call-done, s32[1024]{0:T(1024)S(1)} %pad_clamp_fusion), kind=kCustom, calls=%fused_computation.1 | custom fusion | bytes 4194368 | tf_op jit(solution)/shard_map/jit(_take)/gather | solution.py:99
  164.5 8.1 %all-to-all-start.1 = ((bf16[16,256,256]{2,1,0:T(8,128)(2,1)}), bf16[16,256,256]{2,1,0:T(8,128)(2,1)}, u32[]{:S(2)}, u32[]{:S(2)}) async-start(bf16[16,256,256]{2,1,0:T(8,128)(2,1)} %gather_fusion.1), calls=%async_computation.1 | async-start | bytes 4194304 | tf_op jit(solution)/shard_map/all_to_all | solution.py:100
  172.6 0.1 fusion.19
  172.8 3.5 %collective-permute-start.8 = (bf16[256,256]{1,0:T(8,128)(2,1)S(1)}, bf16[256,256]{1,0:T(8,128)(2,1)S(1)}, u32[]{:S(2)}, u32[]{:S(2)}) collective-permute-start(bf16[256,256]{1,0:T(8,128)(2,1)S(1)} %fusion.16), channel_id=1, source_target_pairs={{0,1},{1,2},{2,3},{3,4},{4,5},{5,6},{6,7},{7,8},{8,9},{9,10},{10,1... | collective-permute-start | bytes 393224 | tf_op jit(solution)/shard_map/ppermute | solution.py:23
  176.3 0.1 constant_dynamic-slice_fusion.1
  176.4 0.5 fusion.43
  180.8 39.0 %collective-permute-done.8 = bf16[256,256]{1,0:T(8,128)(2,1)S(1)} collective-permute-done((bf16[256,256]{1,0:T(8,128)(2,1)S(1)}, bf16[256,256]{1,0:T(8,128)(2,1)S(1)}, u32[]{:S(2)}, u32[]{:S(2)}) %collective-permute-start.8) | collective-permute-done | bytes 131104 | tf_op jit(solution)/shard_map/ppermute | solution.py:23
  219.8 1.7 convolution_bitcast_fusion.2
  221.5 1.4 add_add_fusion
  223.0 1.1 constant_dynamic-slice_fusion
  224.1 5.8 %collective-permute-start.9 = (bf16[512,256]{1,0:T(8,128)(2,1)S(1)}, bf16[512,256]{1,0:T(8,128)(2,1)S(1)}, u32[]{:S(2)}, u32[]{:S(2)}) collective-permute-start(bf16[512,256]{1,0:T(8,128)(2,1)S(1)} %bitcast.101), channel_id=1, source_target_pairs={{0,1},{1,0},{2,3},{3,2},{4,5},{5,4},{6,7},{7,6},{8,9},{9,8},{10,11... | collective-permute-start | bytes 786440 | tf_op jit(solution)/shard_map/ppermute | solution.py:72
  229.9 0.4 convolution_bitcast_fusion.1
  230.3 0.7 collective-permute-done.9
  231.0 0.4 convolution_bitcast_fusion
  231.5 0.8 fusion.18
  232.2 1.4 fusion.1
  233.7 1.6 fusion.13
  235.2 0.8 copy.25
  (25 shorter events, 0.1 us)
Async XLA Ops:
  6.5 78.6 %copy-start = (bf16[256,4096]{1,0:T(8,128)(2,1)S(1)}, bf16[256,4096]{1,0:T(8,128)(2,1)}, u32[]{:S(2)}) copy-start(bf16[256,4096]{1,0:T(8,128)(2,1)} %param.5) | copy-start | bytes 6291460
  6.5 13.6 %copy-start.3 = (bf16[256,512]{1,0:T(8,128)(2,1)S(1)}, bf16[256,512]{1,0:T(8,128)(2,1)}, u32[]{:S(2)}) copy-start(bf16[256,512]{1,0:T(8,128)(2,1)} %param.6) | copy-start | bytes 786436
  9.1 76.1 %all-to-all-start = ((bf16[16,256,256]{2,1,0:T(8,128)(2,1)}), bf16[16,256,256]{2,1,0:T(8,128)(2,1)}, u32[]{:S(2)}, u32[]{:S(2)}) async-start(bf16[16,256,256]{2,1,0:T(8,128)(2,1)} %tile.2), calls=%async_computation | async-start | bytes 4194304 | tf_op jit(solution)/shard_map/all_to_all | solution.py:11
  20.1 140.2 %all-gather.4.cloned.1.call-start = ((), (), s32[]{:S(2)}) async-start(), calls=%async_computation.2 | async-start | bytes 4718592 | tf_op jit(solution)/shard_map/all_gather | solution.py:89
  20.2 54.1 %collective-permute-start = (bf16[256,512]{1,0:T(8,128)(2,1)S(1)}, bf16[256,512]{1,0:T(8,128)(2,1)S(1)}, u32[]{:S(2)}, u32[]{:S(2)}) collective-permute-start(bf16[256,512]{1,0:T(8,128)(2,1)S(1)} %copy-done.3), channel_id=1, source_target_pairs={{0,2},{1,3},{2,4},{3,5},{4,6},{5,7},{6,8},{7,9},{8,10},{9,11},{10,... | collective-permute-start | bytes 786440 | tf_op jit(solution)/shard_map/ppermute | solution.py:47
  23.5 52.7 %collective-permute-start.2 = (bf16[256,512]{1,0:T(8,128)(2,1)S(1)}, bf16[256,512]{1,0:T(8,128)(2,1)S(1)}, u32[]{:S(2)}, u32[]{:S(2)}) collective-permute-start(bf16[256,512]{1,0:T(8,128)(2,1)S(1)} %copy-done.3), channel_id=1, source_target_pairs={{0,14},{1,15},{2,0},{3,1},{4,2},{5,3},{6,4},{7,5},{8,6},{9,7},{10,... | collective-permute-start | bytes 786440 | tf_op jit(solution)/shard_map/ppermute | solution.py:50
  74.2 10.0 %collective-permute-start.1 = (bf16[256,512]{1,0:T(8,128)(2,1)S(1)}, bf16[256,512]{1,0:T(8,128)(2,1)S(1)}, u32[]{:S(2)}, u32[]{:S(2)}) collective-permute-start(bf16[256,512]{1,0:T(8,128)(2,1)S(1)} %collective-permute-done), channel_id=1, source_target_pairs={{0,2},{1,3},{2,4},{3,5},{4,6},{5,7},{6,8},{7,9},{8,10},{9,11},{10,... | collective-permute-start | bytes 786440 | tf_op jit(solution)/shard_map/ppermute | solution.py:47
  76.2 9.0 %collective-permute-start.3 = (bf16[256,512]{1,0:T(8,128)(2,1)S(1)}, bf16[256,512]{1,0:T(8,128)(2,1)S(1)}, u32[]{:S(2)}, u32[]{:S(2)}) collective-permute-start(bf16[256,512]{1,0:T(8,128)(2,1)S(1)} %collective-permute-done.2), channel_id=1, source_target_pairs={{0,14},{1,15},{2,0},{3,1},{4,2},{5,3},{6,4},{7,5},{8,6},{9,7},{10,... | collective-permute-start | bytes 786440 | tf_op jit(solution)/shard_map/ppermute | solution.py:50
  98.8 9.1 %collective-permute-start.4 = (bf16[256,512]{1,0:T(8,128)(2,1)S(1)}, bf16[256,512]{1,0:T(8,128)(2,1)S(1)}, u32[]{:S(2)}, u32[]{:S(2)}) collective-permute-start(bf16[256,512]{1,0:T(8,128)(2,1)S(1)} %collective-permute-done.1), channel_id=1, source_target_pairs={{0,2},{1,3},{2,4},{3,5},{4,6},{5,7},{6,8},{7,9},{8,10},{9,11},{10,... | collective-permute-start | bytes 786440 | tf_op jit(solution)/shard_map/ppermute | solution.py:47
  107.9 15.8 %copy-start.5 = (bf16[256,512]{1,0:T(8,128)(2,1)}, bf16[256,512]{1,0:T(8,128)(2,1)S(1)}, u32[]{:S(2)}) copy-start(bf16[256,512]{1,0:T(8,128)(2,1)S(1)} %collective-permute-done.4) | copy-start | bytes 786436
  107.9 8.3 %collective-permute-start.5 = (bf16[256,512]{1,0:T(8,128)(2,1)S(1)}, bf16[256,512]{1,0:T(8,128)(2,1)S(1)}, u32[]{:S(2)}, u32[]{:S(2)}) collective-permute-start(bf16[256,512]{1,0:T(8,128)(2,1)S(1)} %collective-permute-done.4), channel_id=1, source_target_pairs={{0,2},{1,3},{2,4},{3,5},{4,6},{5,7},{6,8},{7,9},{8,10},{9,11},{10,... | collective-permute-start | bytes 786440 | tf_op jit(solution)/shard_map/ppermute | solution.py:47
  109.8 12.3 %collective-permute-start.6 = (bf16[256,512]{1,0:T(8,128)(2,1)S(1)}, bf16[256,512]{1,0:T(8,128)(2,1)S(1)}, u32[]{:S(2)}, u32[]{:S(2)}) collective-permute-start(bf16[256,512]{1,0:T(8,128)(2,1)S(1)} %collective-permute-done.3), channel_id=1, source_target_pairs={{0,14},{1,15},{2,0},{3,1},{4,2},{5,3},{6,4},{7,5},{8,6},{9,7},{10,... | collective-permute-start | bytes 786440 | tf_op jit(solution)/shard_map/ppermute | solution.py:50
  116.2 7.5 %copy-start.6 = (bf16[256,512]{1,0:T(8,128)(2,1)}, bf16[256,512]{1,0:T(8,128)(2,1)S(1)}, u32[]{:S(2)}) copy-start(bf16[256,512]{1,0:T(8,128)(2,1)S(1)} %collective-permute-done.5) | copy-start | bytes 786436
  122.1 0.7 copy-start.4
  123.7 17.1 %collective-permute-start.7 = (bf16[8,256,512]{2,1,0:T(8,128)(2,1)}, bf16[8,256,512]{2,1,0:T(8,128)(2,1)}, u32[]{:S(2)}, u32[]{:S(2)}) collective-permute-start(bf16[8,256,512]{2,1,0:T(8,128)(2,1)} %get-tuple-element.17), channel_id=1, source_target_pairs={{0,1},{1,0},{2,3},{3,2},{4,5},{5,4},{6,7},{7,6},{8,9},{9,8},{10,11... | collective-permute-start | bytes 6291464 | tf_op jit(solution)/shard_map/ppermute | solution.py:53
  145.8 1.3 copy-start.1
  164.5 58.4 %all-to-all-start.1 = ((bf16[16,256,256]{2,1,0:T(8,128)(2,1)}), bf16[16,256,256]{2,1,0:T(8,128)(2,1)}, u32[]{:S(2)}, u32[]{:S(2)}) async-start(bf16[16,256,256]{2,1,0:T(8,128)(2,1)} %gather_fusion.1), calls=%async_computation.1 | async-start | bytes 4194304 | tf_op jit(solution)/shard_map/all_to_all | solution.py:100
  172.8 47.0 %collective-permute-start.8 = (bf16[256,256]{1,0:T(8,128)(2,1)S(1)}, bf16[256,256]{1,0:T(8,128)(2,1)S(1)}, u32[]{:S(2)}, u32[]{:S(2)}) collective-permute-start(bf16[256,256]{1,0:T(8,128)(2,1)S(1)} %fusion.16), channel_id=1, source_target_pairs={{0,1},{1,2},{2,3},{3,4},{4,5},{5,6},{6,7},{7,8},{8,9},{9,10},{10,1... | collective-permute-start | bytes 393224 | tf_op jit(solution)/shard_map/ppermute | solution.py:23
  223.0 8.5 %copy-start.2 = (f32[4,256,512]{1,2,0:T(8,128)S(1)}, f32[4,256,512]{1,2,0:T(8,128)}, u32[]{:S(2)}) copy-start(f32[4,256,512]{1,2,0:T(8,128)} %convolution_bitcast_fusion.2) | copy-start | bytes 6291460
  224.1 6.9 %collective-permute-start.9 = (bf16[512,256]{1,0:T(8,128)(2,1)S(1)}, bf16[512,256]{1,0:T(8,128)(2,1)S(1)}, u32[]{:S(2)}, u32[]{:S(2)}) collective-permute-start(bf16[512,256]{1,0:T(8,128)(2,1)S(1)} %bitcast.101), channel_id=1, source_target_pairs={{0,1},{1,0},{2,3},{3,2},{4,5},{5,4},{6,7},{7,6},{8,9},{9,8},{10,11... | collective-permute-start | bytes 786440 | tf_op jit(solution)/shard_map/ppermute | solution.py:72
Sparse Core Ops, SparseCore 0:
  98.9 61.3 all-gather.3
